TPU v7x, 32 devices: a whole 2x2x4 slice. The times are simulated.
32 devices in a mesh: groups: 2 (over x), tm: 16 (over z, y, core).
Axes of the slice: x: 2, y: 2, z: 4, core: 2. Of those that a mesh axis runs over, the one named last changes fastest.
Arguments:
- feats: bfloat16 [32, 16, 32, 128], P(('groups', 'tm')), parts along dimension 0, may hold values from -6 to 6
- clip_lengths: int32 [8], P('groups'), parts along dimension 0, may hold values from 1 to 8, 16 in all
- reversed_clip: int32 [8], P('groups'), parts along dimension 0, may hold values 0 or 1
- merge_weight: bfloat16 [2, 3, 3, 256, 128], replicated, may hold values from -0.125 to 0.125
- block_weight: bfloat16 [2, 4, 3, 3, 128, 128], replicated, may hold values from -0.1875 to 0.1875
- out_weight: bfloat16 [256, 128], replicated, may hold values from -0.375 to 0.375
Outputs:
- merged: bfloat16 [32, 16, 32, 128], P(('groups', 'tm')), parts along dimension 0
There are 2 independent parts, one for each index of `groups`. A program takes and returns all parts, laid end to end along the dimension named above; an argument that names none is the same for every part. Nothing has to cross between parts.
Inputs may be any that keep to these rules, and one draw needn't show every extreme that they name: `clip_lengths`: each clip holds 1 to 8 frames, the clips fill all 16 frames in order, one holds exactly 8.
All inputs are finite; a program needn't handle non-finite values.
Results may differ from a plain program's by a relative error of at most 0.018.
Values may be sent and summed in bfloat16 or wider, within the bound.
No kernel may reach another device: no remote copies, remote signals or barrier semaphores. Data moves between devices by JAX's collectives and lax.ppermute only.
A program may use at most 64 MiB of HBM per device.

v0:
```python
import jax
import jax.numpy as jnp
from jax import lax
from jax.sharding import PartitionSpec as P

CLIP = 8


def shifted(x, axis, by):
    devices = lax.axis_size(axis)
    pairs = [(i, i + by) for i in range(devices) if 0 <= i + by < devices]
    return lax.ppermute(x, axis, pairs)


def conv_tile(x, w):
    rows, cols, inner = x.shape
    padded = jnp.pad(x, ((1, 1), (1, 1), (0, 0)))
    pieces = []
    for i in range(3):
        for j in range(3):
            pieces.append(padded[i : i + rows, j : j + cols].reshape(rows * cols, inner))
    joined = jnp.concatenate(pieces, -1)
    acc = jnp.dot(joined, w.reshape(9 * inner, w.shape[-1]), preferred_element_type=jnp.float32)
    return acc.reshape(rows, cols, -1)


def recur_step(prev, feat, merge_w, block_w):
    y = conv_tile(jnp.concatenate([prev, feat], -1), merge_w)
    y = jnp.where(y > 0, y, 0.1 * y).astype(jnp.bfloat16)
    for blk in range(2):
        z = jnp.maximum(conv_tile(y, block_w[2 * blk]), 0.0).astype(jnp.bfloat16)
        y = (y.astype(jnp.float32) + conv_tile(z, block_w[2 * blk + 1])).astype(jnp.bfloat16)
    return y


def frame_flags(frame_ids, clip_lengths, reversed_clip):
    ends = jnp.cumsum(clip_lengths)
    starts = ends - clip_lengths
    is_start = jnp.any(frame_ids[:, None] == starts[None], 1)
    is_last = jnp.any(frame_ids[:, None] + 1 == ends[None], 1)
    clip_of = jnp.sum((ends[None] <= frame_ids[:, None]).astype(jnp.int32), 1)
    clip_ids = jnp.arange(clip_lengths.shape[0], dtype=jnp.int32)
    rev = jnp.sum(jnp.where(clip_ids[None] == clip_of[:, None], reversed_clip[None], 0), 1)
    return (is_start, is_last, rev)


def on_device(feats, clip_lengths, reversed_clip, merge_weight, block_weight, out_weight):
    span = CLIP
    here = lax.axis_index("tm")
    feat = feats[0]
    zero = jnp.zeros(feat.shape, jnp.bfloat16)
    own_start, own_last, own_rev = frame_flags(jnp.reshape(here, (1,)), clip_lengths, reversed_clip)
    back = own_rev[0]
    merge_a = lax.dynamic_index_in_dim(merge_weight, back, 0, keepdims=False)
    block_a = lax.dynamic_index_in_dim(block_weight, back, 0, keepdims=False)
    merge_b = lax.dynamic_index_in_dim(merge_weight, 1 - back, 0, keepdims=False)
    block_b = lax.dynamic_index_in_dim(block_weight, 1 - back, 0, keepdims=False)

    def tick(_, carry):
        state_a, state_b = carry
        recv_a = shifted(state_a, "tm", 1)
        recv_b = shifted(state_b, "tm", -1)
        recv_a = jnp.where(own_start[0], zero, recv_a)
        recv_b = jnp.where(own_last[0], zero, recv_b)
        return (
            recur_step(recv_a, feat, merge_a, block_a),
            recur_step(recv_b, feat, merge_b, block_b),
        )

    chain_a, chain_b = lax.fori_loop(0, span, tick, (zero, zero))
    forward = jnp.where(back > 0, chain_b, chain_a)
    backward = jnp.where(back > 0, chain_a, chain_b)
    both = jnp.concatenate([forward, backward], -1).reshape(-1, out_weight.shape[0])
    merged = jnp.dot(both, out_weight, preferred_element_type=jnp.float32)
    return merged.reshape(feats.shape).astype(jnp.bfloat16)


def solution(mesh):
    return jax.shard_map(
        on_device,
        mesh=mesh,
        in_specs=(P(("groups", "tm"), None, None, None), P("groups"), P("groups"), P(), P(), P()),
        out_specs=P(("groups", "tm"), None, None, None),
        check_vma=False,
    )
```

profile of v0, /device:TPU:10, one launch (start us, length us, event | category | flops | bytes accessed | tf_op | source)
XLA Modules:
  0.0 276.7 jit_solution(2466940939306392671)
XLA Ops:
  1.5 1.9 fusion.32
  6.6 2.0 dynamic-slice_bitcast_fusion
  11.1 263.0 %while.15 = (s32[]{:T(128)}, bf16[16,32,128]{2,1,0:T(8,128)(2,1)}, bf16[16,32,128]{2,1,0:T(8,128)(2,1)}, pred[1]{0:T(512)(128)(4,1)}, bf16[16,32,128]{2,1,0:T(8,...) while((s32[]{:T(128)}, bf16[16,32,128]{2,1,0:T(8,128)(2,1)}, ...), condition=%wide.region_6.7_spmd.clone, body=%wide.region_5.6_spmd.clone.sunk | while | flops 1815085056 | bytes 66060696 | solution.py:70
  11.8 2.7 collective-permute-start
  15.2 1.9 collective-permute-start.1
  19.8 2.9 %collective-permute-done.1 = bf16[16,32,128]{2,1,0:T(8,128)(2,1)} collective-permute-done((bf16[16,32,128]{2,1,0:T(8,128)(2,1)}, bf16[16,32,128]{2,1,0:T(8,128)(2,1)}, u32[]{:S(2)}, u32[]{:S(2)}) %collective-permute-start.1) | collective-permute-done | bytes 131104 | tf_op jit(solution)/shard_map/while/body/eval_jaxpr/ppermute | solution.py:12
  44.7 1.9 collective-permute-start
  48.2 2.4 collective-permute-start.1
  53.3 2.4 collective-permute-done.1
  77.7 1.9 collective-permute-start
  81.2 2.4 collective-permute-start.1
  86.3 2.4 collective-permute-done.1
  114.2 2.4 collective-permute-start.1
  119.3 2.4 collective-permute-done.1
  147.2 2.4 collective-permute-start.1
  152.3 2.4 collective-permute-done.1
  176.7 1.9 collective-permute-start
  180.2 2.4 collective-permute-start.1
  185.3 2.4 collective-permute-done.1
  209.7 1.9 collective-permute-start
  213.2 2.4 collective-permute-start.1
  218.3 2.4 collective-permute-done.1
  246.2 2.4 collective-permute-start.1
  251.3 2.4 collective-permute-done.1
  (988 shorter events, 216.0 us)
Async XLA Ops:
  0.0 275.8 %copy-start = (bf16[256,128]{1,0:T(8,128)(2,1)S(1)}, bf16[256,128]{1,0:T(8,128)(2,1)}, u32[]{:S(2)}) copy-start(bf16[256,128]{1,0:T(8,128)(2,1)} %param.13) | copy-start | bytes 196612
  6.6 2.0 copy-start.7
  8.6 1.8 copy-start.10
  8.6 2.5 copy-start.6
  11.8 6.6 %collective-permute-start = (bf16[16,32,128]{2,1,0:T(8,128)(2,1)}, bf16[16,32,128]{2,1,0:T(8,128)(2,1)}, u32[]{:S(2)}, u32[]{:S(2)}) collective-permute-start(bf16[16,32,128]{2,1,0:T(8,128)(2,1)} %broadcast_select_fusion.10), channel_id=1, source_target_pairs={{1,0},{2,1},{3,2},{4,3},{5,4},{6,5},{7,6},{8,7},{9,8},{10,9},{11,1... | collective-permute-start | bytes 393224 | tf_op jit(solution)/shard_map/while/body/eval_jaxpr/ppermute | solution.py:12
  15.2 7.5 %collective-permute-start.1 = (bf16[16,32,128]{2,1,0:T(8,128)(2,1)}, bf16[16,32,128]{2,1,0:T(8,128)(2,1)}, u32[]{:S(2)}, u32[]{:S(2)}) collective-permute-start(bf16[16,32,128]{2,1,0:T(8,128)(2,1)} %broadcast_select_fusion.12), channel_id=1, source_target_pairs={{0,1},{1,2},{2,3},{3,4},{4,5},{5,6},{6,7},{7,8},{8,9},{9,10},{10,1... | collective-permute-start | bytes 393224 | tf_op jit(solution)/shard_map/while/body/eval_jaxpr/ppermute | solution.py:12
  28.1 1.1 copy-start.8
  44.7 7.1 %collective-permute-start = (bf16[16,32,128]{2,1,0:T(8,128)(2,1)}, bf16[16,32,128]{2,1,0:T(8,128)(2,1)}, u32[]{:S(2)}, u32[]{:S(2)}) collective-permute-start(bf16[16,32,128]{2,1,0:T(8,128)(2,1)} %broadcast_select_fusion.10), channel_id=1, source_target_pairs={{1,0},{2,1},{3,2},{4,3},{5,4},{6,5},{7,6},{8,7},{9,8},{10,9},{11,1... | collective-permute-start | bytes 393224 | tf_op jit(solution)/shard_map/while/body/eval_jaxpr/ppermute | solution.py:12
  48.2 7.5 %collective-permute-start.1 = (bf16[16,32,128]{2,1,0:T(8,128)(2,1)}, bf16[16,32,128]{2,1,0:T(8,128)(2,1)}, u32[]{:S(2)}, u32[]{:S(2)}) collective-permute-start(bf16[16,32,128]{2,1,0:T(8,128)(2,1)} %broadcast_select_fusion.12), channel_id=1, source_target_pairs={{0,1},{1,2},{2,3},{3,4},{4,5},{5,6},{6,7},{7,8},{8,9},{9,10},{10,1... | collective-permute-start | bytes 393224 | tf_op jit(solution)/shard_map/while/body/eval_jaxpr/ppermute | solution.py:12
  61.1 1.1 copy-start.8
  67.7 1.1 copy-start.9
  77.7 7.1 %collective-permute-start = (bf16[16,32,128]{2,1,0:T(8,128)(2,1)}, bf16[16,32,128]{2,1,0:T(8,128)(2,1)}, u32[]{:S(2)}, u32[]{:S(2)}) collective-permute-start(bf16[16,32,128]{2,1,0:T(8,128)(2,1)} %broadcast_select_fusion.10), channel_id=1, source_target_pairs={{1,0},{2,1},{3,2},{4,3},{5,4},{6,5},{7,6},{8,7},{9,8},{10,9},{11,1... | collective-permute-start | bytes 393224 | tf_op jit(solution)/shard_map/while/body/eval_jaxpr/ppermute | solution.py:12
  81.2 7.5 %collective-permute-start.1 = (bf16[16,32,128]{2,1,0:T(8,128)(2,1)}, bf16[16,32,128]{2,1,0:T(8,128)(2,1)}, u32[]{:S(2)}, u32[]{:S(2)}) collective-permute-start(bf16[16,32,128]{2,1,0:T(8,128)(2,1)} %broadcast_select_fusion.12), channel_id=1, source_target_pairs={{0,1},{1,2},{2,3},{3,4},{4,5},{5,6},{6,7},{7,8},{8,9},{9,10},{10,1... | collective-permute-start | bytes 393224 | tf_op jit(solution)/shard_map/while/body/eval_jaxpr/ppermute | solution.py:12
  110.7 7.1 %collective-permute-start = (bf16[16,32,128]{2,1,0:T(8,128)(2,1)}, bf16[16,32,128]{2,1,0:T(8,128)(2,1)}, u32[]{:S(2)}, u32[]{:S(2)}) collective-permute-start(bf16[16,32,128]{2,1,0:T(8,128)(2,1)} %broadcast_select_fusion.10), channel_id=1, source_target_pairs={{1,0},{2,1},{3,2},{4,3},{5,4},{6,5},{7,6},{8,7},{9,8},{10,9},{11,1... | collective-permute-start | bytes 393224 | tf_op jit(solution)/shard_map/while/body/eval_jaxpr/ppermute | solution.py:12
  114.2 7.5 %collective-permute-start.1 = (bf16[16,32,128]{2,1,0:T(8,128)(2,1)}, bf16[16,32,128]{2,1,0:T(8,128)(2,1)}, u32[]{:S(2)}, u32[]{:S(2)}) collective-permute-start(bf16[16,32,128]{2,1,0:T(8,128)(2,1)} %broadcast_select_fusion.12), channel_id=1, source_target_pairs={{0,1},{1,2},{2,3},{3,4},{4,5},{5,6},{6,7},{7,8},{8,9},{9,10},{10,1... | collective-permute-start | bytes 393224 | tf_op jit(solution)/shard_map/while/body/eval_jaxpr/ppermute | solution.py:12
  143.7 7.1 %collective-permute-start = (bf16[16,32,128]{2,1,0:T(8,128)(2,1)}, bf16[16,32,128]{2,1,0:T(8,128)(2,1)}, u32[]{:S(2)}, u32[]{:S(2)}) collective-permute-start(bf16[16,32,128]{2,1,0:T(8,128)(2,1)} %broadcast_select_fusion.10), channel_id=1, source_target_pairs={{1,0},{2,1},{3,2},{4,3},{5,4},{6,5},{7,6},{8,7},{9,8},{10,9},{11,1... | collective-permute-start | bytes 393224 | tf_op jit(solution)/shard_map/while/body/eval_jaxpr/ppermute | solution.py:12
  147.2 7.5 %collective-permute-start.1 = (bf16[16,32,128]{2,1,0:T(8,128)(2,1)}, bf16[16,32,128]{2,1,0:T(8,128)(2,1)}, u32[]{:S(2)}, u32[]{:S(2)}) collective-permute-start(bf16[16,32,128]{2,1,0:T(8,128)(2,1)} %broadcast_select_fusion.12), channel_id=1, source_target_pairs={{0,1},{1,2},{2,3},{3,4},{4,5},{5,6},{6,7},{7,8},{8,9},{9,10},{10,1... | collective-permute-start | bytes 393224 | tf_op jit(solution)/shard_map/while/body/eval_jaxpr/ppermute | solution.py:12
  176.7 7.1 %collective-permute-start = (bf16[16,32,128]{2,1,0:T(8,128)(2,1)}, bf16[16,32,128]{2,1,0:T(8,128)(2,1)}, u32[]{:S(2)}, u32[]{:S(2)}) collective-permute-start(bf16[16,32,128]{2,1,0:T(8,128)(2,1)} %broadcast_select_fusion.10), channel_id=1, source_target_pairs={{1,0},{2,1},{3,2},{4,3},{5,4},{6,5},{7,6},{8,7},{9,8},{10,9},{11,1... | collective-permute-start | bytes 393224 | tf_op jit(solution)/shard_map/while/body/eval_jaxpr/ppermute | solution.py:12
  180.2 7.5 %collective-permute-start.1 = (bf16[16,32,128]{2,1,0:T(8,128)(2,1)}, bf16[16,32,128]{2,1,0:T(8,128)(2,1)}, u32[]{:S(2)}, u32[]{:S(2)}) collective-permute-start(bf16[16,32,128]{2,1,0:T(8,128)(2,1)} %broadcast_select_fusion.12), channel_id=1, source_target_pairs={{0,1},{1,2},{2,3},{3,4},{4,5},{5,6},{6,7},{7,8},{8,9},{9,10},{10,1... | collective-permute-start | bytes 393224 | tf_op jit(solution)/shard_map/while/body/eval_jaxpr/ppermute | solution.py:12
  199.7 1.1 copy-start.9
  209.7 7.1 %collective-permute-start = (bf16[16,32,128]{2,1,0:T(8,128)(2,1)}, bf16[16,32,128]{2,1,0:T(8,128)(2,1)}, u32[]{:S(2)}, u32[]{:S(2)}) collective-permute-start(bf16[16,32,128]{2,1,0:T(8,128)(2,1)} %broadcast_select_fusion.10), channel_id=1, source_target_pairs={{1,0},{2,1},{3,2},{4,3},{5,4},{6,5},{7,6},{8,7},{9,8},{10,9},{11,1... | collective-permute-start | bytes 393224 | tf_op jit(solution)/shard_map/while/body/eval_jaxpr/ppermute | solution.py:12
  213.2 7.5 %collective-permute-start.1 = (bf16[16,32,128]{2,1,0:T(8,128)(2,1)}, bf16[16,32,128]{2,1,0:T(8,128)(2,1)}, u32[]{:S(2)}, u32[]{:S(2)}) collective-permute-start(bf16[16,32,128]{2,1,0:T(8,128)(2,1)} %broadcast_select_fusion.12), channel_id=1, source_target_pairs={{0,1},{1,2},{2,3},{3,4},{4,5},{5,6},{6,7},{7,8},{8,9},{9,10},{10,1... | collective-permute-start | bytes 393224 | tf_op jit(solution)/shard_map/while/body/eval_jaxpr/ppermute | solution.py:12
  242.7 7.1 %collective-permute-start = (bf16[16,32,128]{2,1,0:T(8,128)(2,1)}, bf16[16,32,128]{2,1,0:T(8,128)(2,1)}, u32[]{:S(2)}, u32[]{:S(2)}) collective-permute-start(bf16[16,32,128]{2,1,0:T(8,128)(2,1)} %broadcast_select_fusion.10), channel_id=1, source_target_pairs={{1,0},{2,1},{3,2},{4,3},{5,4},{6,5},{7,6},{8,7},{9,8},{10,9},{11,1... | collective-permute-start | bytes 393224 | tf_op jit(solution)/shard_map/while/body/eval_jaxpr/ppermute | solution.py:12
  246.2 7.5 %collective-permute-start.1 = (bf16[16,32,128]{2,1,0:T(8,128)(2,1)}, bf16[16,32,128]{2,1,0:T(8,128)(2,1)}, u32[]{:S(2)}, u32[]{:S(2)}) collective-permute-start(bf16[16,32,128]{2,1,0:T(8,128)(2,1)} %broadcast_select_fusion.12), channel_id=1, source_target_pairs={{0,1},{1,2},{2,3},{3,4},{4,5},{5,6},{6,7},{7,8},{8,9},{9,10},{10,1... | collective-permute-start | bytes 393224 | tf_op jit(solution)/shard_map/while/body/eval_jaxpr/ppermute | solution.py:12
  (52 other events, 51.3 us)
where the time goes:
time: 281 us; the launch traced here: 277 us
  local copies, waits for them, and re-layouts  79.9 us (28%)
  other arithmetic  79.9 us (28%)
  matrix products  54.4 us (19%)
  starting transfers between devices  34.8 us (12%)
  waiting for transfers between devices  19.5 us (7%)
  loops' own time  4.39 us (2%)
  between operations  3.79 us (1%)
    while x736, local copies, waits for them, and re-layouts  62.2 us
    dot_general x80, matrix products, conv_tile(): jnp.dot(joined, w.reshape(9 * inner, w.shape[-1]), preferred_element_type...  53.5 us
    while x32, other arithmetic  48.8 us
    ppermute x16, starting transfers between devices, shifted(): return lax.ppermute(x, axis, pairs)  34.8 us
    ppermute x16, waiting for transfers between devices, shifted(): return lax.ppermute(x, axis, pairs)  19.5 us
    select_n x8, other arithmetic, tick(): recv_a = jnp.where(own_start[0], zero, recv_a)  12.9 us
    select_n x8, other arithmetic, tick(): recv_b = jnp.where(own_last[0], zero, recv_b)  12 us
    slice x8, local copies, waits for them, and re-layouts, recur_step(): block_w[2 * blk + 1]  9.67 us
  transfers between devices with their start and end apart: 16, of which 8 were waited for; matrix products, arithmetic and copies ran while one was open for 12% of the time, Pallas kernels for 0%

commit v1 on v0

--- a/solution.py
+++ b/solution.py
@@ -13,15 +13,12 @@
 
 
 def conv_tile(x, w):
-    rows, cols, inner = x.shape
-    padded = jnp.pad(x, ((1, 1), (1, 1), (0, 0)))
-    pieces = []
-    for i in range(3):
-        for j in range(3):
-            pieces.append(padded[i : i + rows, j : j + cols].reshape(rows * cols, inner))
-    joined = jnp.concatenate(pieces, -1)
-    acc = jnp.dot(joined, w.reshape(9 * inner, w.shape[-1]), preferred_element_type=jnp.float32)
-    return acc.reshape(rows, cols, -1)
+    out = lax.conv_general_dilated(
+        x[None], w, (1, 1), ((1, 1), (1, 1)),
+        dimension_numbers=("NHWC", "HWIO", "NHWC"),
+        preferred_element_type=jnp.float32,
+    )
+    return out[0]
 
 
 def recur_step(prev, feat, merge_w, block_w):

time: 281 us -> 167 us (0.59)
  local copies, waits for them, and re-layouts: 79.9 us -> 19.7 us
  other arithmetic: 79.9 us -> 19.8 us
  waiting for transfers between devices: 19.5 us -> 33.1 us
  matrix products: 54.4 us -> 51.2 us
    dot_general x80 -> x0, matrix products: 53.5 us -> none  [conv_tile(): jnp.dot(joined, w.reshape(9 * inner, w.shape[-1]), preferred_element_type...]
    while x736 -> x32, local copies, waits for them, and re-layouts: 62.2 us -> 9.86 us
    conv_general_dilated x0 -> x80, matrix products: none -> 50.3 us  [conv_tile(): lax.conv_general_dilated(x[None], w, (1, 1), ((1, 1), (1, 1)), dimension_...]
    while x32 -> x16, other arithmetic: 48.8 us -> 0.24 us
    ppermute x16, waiting for transfers between devices: 19.5 us -> 33.1 us  [shifted(): return lax.ppermute(x, axis, pairs)]
    slice x8 -> x0, local copies, waits for them, and re-layouts: 9.67 us -> none  [recur_step(): block_w[2 * blk + 1]]
    select_n x8, other arithmetic: 12.9 us -> 5.1 us  [tick(): recv_a = jnp.where(own_start[0], zero, recv_a)]
    select_n x8, other arithmetic: 12 us -> 5.5 us  [tick(): recv_b = jnp.where(own_last[0], zero, recv_b)]
  transfers between devices with their start and end apart: 16 -> 16, of which waited for: 8 -> 16; matrix products, arithmetic and copies ran while one was open for 12% -> 3% of each run, Pallas kernels for 0% -> 0%
where the time goes in v1:
time: 167 us; the launch traced here: 165 us
  matrix products  51.2 us (31%)
  starting transfers between devices  35 us (21%)
  waiting for transfers between devices  33.1 us (20%)
  other arithmetic  19.8 us (12%)
  local copies, waits for them, and re-layouts  19.7 us (12%)
  between operations  3.88 us (2%)
  loops' own time  2.58 us (2%)
    conv_general_dilated x80, matrix products, conv_tile(): lax.conv_general_dilated(x[None], w, (1, 1), ((1, 1), (1, 1)), dimension_...  50.3 us
    ppermute x16, starting transfers between devices, shifted(): return lax.ppermute(x, axis, pairs)  35 us
    ppermute x16, waiting for transfers between devices, shifted(): return lax.ppermute(x, axis, pairs)  33.1 us
    while x32, local copies, waits for them, and re-layouts  9.86 us
    select_n x8, other arithmetic, tick(): recv_b = jnp.where(own_last[0], zero, recv_b)  5.5 us
    conv_general_dilated x80, local copies, waits for them, and re-layouts, conv_tile(): lax.conv_general_dilated(x[None], w, (1, 1), ((1, 1), (1, 1)), dimension_...  5.26 us
    select_n x8, other arithmetic, tick(): recv_a = jnp.where(own_start[0], zero, recv_a)  5.1 us
  transfers between devices with their start and end apart: 16, of which 16 were waited for; matrix products, arithmetic and copies ran while one was open for 3% of the time, Pallas kernels for 0%

profile of v1, /device:TPU:10, one launch (start us, length us, event | category | flops | bytes accessed | tf_op | source)
XLA Modules:
  0.0 165.3 jit_solution(15168039966850233259)
XLA Ops:
  1.5 2.0 %fusion.214 = s32[]{:T(128)} fusion(s32[4]{0:T(128)} %param.10, s32[]{:T(128)} %fusion.213), kind=kLoop, calls=%fused_computation.237 | loop fusion | flops 11 | bytes 24 | tf_op jit(solution)/shard_map/reduce_sum | solution.py:40
  6.6 2.0 %dynamic-slice_bitcast_fusion = (bf16[4,3,3,128,128]{4,3,2,1,0:T(8,128)(2,1)S(1)}, bf16[4,3,3,128,128]{4,3,2,1,0:T(8,128)(2,1)S(1)}) fusion(bf16[2,4,3,3,128,128]{5,4,3,2,1,0:T(8,128)(2,1)} %param.12, s32[]{:T(128)S(6)} %select_n.57, s32[]{:T(128)S(6)} %select_n.56), kind=kLoop, calls=%fused_computation.219 | loop fusion | bytes 4718600 | tf_op jit(solution)/shard_map/jit(dynamic_index_in_dim)/squeeze | solution.py:54
  11.2 152.5 %while.13 = (s32[]{:T(128)}, bf16[16,32,128]{2,0,1:T(8,128)(2,1)S(1)}, bf16[16,32,128]{2,0,1:T(8,128)(2,1)S(1)}, pred[1]{0:T(512)(128)(4,1)}, bf16[16,32,128]{2,...) while((s32[]{:T(128)}, ...), condition=%wide.region_6.7_spmd.clone, body=%wide.region_5.6_spmd.clone.sunk | while | flops 2188247040 | bytes 28873188 | solution.py:67
  11.3 2.8 %collective-permute-start = (bf16[16,32,128]{2,0,1:T(8,128)(2,1)S(1)}, bf16[16,32,128]{2,0,1:T(8,128)(2,1)S(1)}, u32[]{:S(2)}, u32[]{:S(2)}) collective-permute-start(bf16[16,32,128]{2,0,1:T(8,128)(2,1)S(1)} %broadcast_select_fusion.10), channel_id=1, source_target_pairs={{1,0},{2,1},{3,2},{4,3},{5,4},{6,5},{7,6},{8,7},{9,8},{10,9},{11,1... | collective-permute-start | bytes 393224 | tf_op jit(solution)/shard_map/while/body/eval_jaxpr/ppermute | solution.py:12
  14.1 1.9 %collective-permute-start.1 = (bf16[16,32,128]{2,0,1:T(8,128)(2,1)S(1)}, bf16[16,32,128]{2,0,1:T(8,128)(2,1)S(1)}, u32[]{:S(2)}, u32[]{:S(2)}) collective-permute-start(bf16[16,32,128]{2,0,1:T(8,128)(2,1)S(1)} %broadcast_select_fusion.12), channel_id=1, source_target_pairs={{0,1},{1,2},{2,3},{3,4},{4,5},{5,6},{6,7},{7,8},{8,9},{9,10},{10,1... | collective-permute-start | bytes 393224 | tf_op jit(solution)/shard_map/while/body/eval_jaxpr/ppermute | solution.py:12
  17.2 4.0 %collective-permute-done.1 = bf16[16,32,128]{2,0,1:T(8,128)(2,1)S(1)} collective-permute-done((bf16[16,32,128]{2,0,1:T(8,128)(2,1)S(1)}, bf16[16,32,128]{2,0,1:T(8,128)(2,1)S(1)}, u32[]{:S(2)}, u32[]{:S(2)}) %collective-permute-start.1) | collective-permute-done | bytes 131104 | tf_op jit(solution)/shard_map/while/body/eval_jaxpr/ppermute | solution.py:12
  31.1 1.9 %collective-permute-start = (bf16[16,32,128]{2,0,1:T(8,128)(2,1)S(1)}, bf16[16,32,128]{2,0,1:T(8,128)(2,1)S(1)}, u32[]{:S(2)}, u32[]{:S(2)}) collective-permute-start(bf16[16,32,128]{2,0,1:T(8,128)(2,1)S(1)} %broadcast_select_fusion.10), channel_id=1, source_target_pairs={{1,0},{2,1},{3,2},{4,3},{5,4},{6,5},{7,6},{8,7},{9,8},{10,9},{11,1... | collective-permute-start | bytes 393224 | tf_op jit(solution)/shard_map/while/body/eval_jaxpr/ppermute | solution.py:12
  33.0 2.4 %collective-permute-start.1 = (bf16[16,32,128]{2,0,1:T(8,128)(2,1)S(1)}, bf16[16,32,128]{2,0,1:T(8,128)(2,1)S(1)}, u32[]{:S(2)}, u32[]{:S(2)}) collective-permute-start(bf16[16,32,128]{2,0,1:T(8,128)(2,1)S(1)} %broadcast_select_fusion.12), channel_id=1, source_target_pairs={{0,1},{1,2},{2,3},{3,4},{4,5},{5,6},{6,7},{7,8},{8,9},{9,10},{10,1... | collective-permute-start | bytes 393224 | tf_op jit(solution)/shard_map/while/body/eval_jaxpr/ppermute | solution.py:12
  36.2 4.0 %collective-permute-done.1 = bf16[16,32,128]{2,0,1:T(8,128)(2,1)S(1)} collective-permute-done((bf16[16,32,128]{2,0,1:T(8,128)(2,1)S(1)}, bf16[16,32,128]{2,0,1:T(8,128)(2,1)S(1)}, u32[]{:S(2)}, u32[]{:S(2)}) %collective-permute-start.1) | collective-permute-done | bytes 131104 | tf_op jit(solution)/shard_map/while/body/eval_jaxpr/ppermute | solution.py:12
  50.0 1.9 %collective-permute-start = (bf16[16,32,128]{2,0,1:T(8,128)(2,1)S(1)}, bf16[16,32,128]{2,0,1:T(8,128)(2,1)S(1)}, u32[]{:S(2)}, u32[]{:S(2)}) collective-permute-start(bf16[16,32,128]{2,0,1:T(8,128)(2,1)S(1)} %broadcast_select_fusion.10), channel_id=1, source_target_pairs={{1,0},{2,1},{3,2},{4,3},{5,4},{6,5},{7,6},{8,7},{9,8},{10,9},{11,1... | collective-permute-start | bytes 393224 | tf_op jit(solution)/shard_map/while/body/eval_jaxpr/ppermute | solution.py:12
  52.0 2.4 %collective-permute-start.1 = (bf16[16,32,128]{2,0,1:T(8,128)(2,1)S(1)}, bf16[16,32,128]{2,0,1:T(8,128)(2,1)S(1)}, u32[]{:S(2)}, u32[]{:S(2)}) collective-permute-start(bf16[16,32,128]{2,0,1:T(8,128)(2,1)S(1)} %broadcast_select_fusion.12), channel_id=1, source_target_pairs={{0,1},{1,2},{2,3},{3,4},{4,5},{5,6},{6,7},{7,8},{8,9},{9,10},{10,1... | collective-permute-start | bytes 393224 | tf_op jit(solution)/shard_map/while/body/eval_jaxpr/ppermute | solution.py:12
  55.1 4.0 %collective-permute-done.1 = bf16[16,32,128]{2,0,1:T(8,128)(2,1)S(1)} collective-permute-done((bf16[16,32,128]{2,0,1:T(8,128)(2,1)S(1)}, bf16[16,32,128]{2,0,1:T(8,128)(2,1)S(1)}, u32[]{:S(2)}, u32[]{:S(2)}) %collective-permute-start.1) | collective-permute-done | bytes 131104 | tf_op jit(solution)/shard_map/while/body/eval_jaxpr/ppermute | solution.py:12
  69.0 1.9 %collective-permute-start = (bf16[16,32,128]{2,0,1:T(8,128)(2,1)S(1)}, bf16[16,32,128]{2,0,1:T(8,128)(2,1)S(1)}, u32[]{:S(2)}, u32[]{:S(2)}) collective-permute-start(bf16[16,32,128]{2,0,1:T(8,128)(2,1)S(1)} %broadcast_select_fusion.10), channel_id=1, source_target_pairs={{1,0},{2,1},{3,2},{4,3},{5,4},{6,5},{7,6},{8,7},{9,8},{10,9},{11,1... | collective-permute-start | bytes 393224 | tf_op jit(solution)/shard_map/while/body/eval_jaxpr/ppermute | solution.py:12
  70.9 2.4 %collective-permute-start.1 = (bf16[16,32,128]{2,0,1:T(8,128)(2,1)S(1)}, bf16[16,32,128]{2,0,1:T(8,128)(2,1)S(1)}, u32[]{:S(2)}, u32[]{:S(2)}) collective-permute-start(bf16[16,32,128]{2,0,1:T(8,128)(2,1)S(1)} %broadcast_select_fusion.12), channel_id=1, source_target_pairs={{0,1},{1,2},{2,3},{3,4},{4,5},{5,6},{6,7},{7,8},{8,9},{9,10},{10,1... | collective-permute-start | bytes 393224 | tf_op jit(solution)/shard_map/while/body/eval_jaxpr/ppermute | solution.py:12
  74.1 4.0 %collective-permute-done.1 = bf16[16,32,128]{2,0,1:T(8,128)(2,1)S(1)} collective-permute-done((bf16[16,32,128]{2,0,1:T(8,128)(2,1)S(1)}, bf16[16,32,128]{2,0,1:T(8,128)(2,1)S(1)}, u32[]{:S(2)}, u32[]{:S(2)}) %collective-permute-start.1) | collective-permute-done | bytes 131104 | tf_op jit(solution)/shard_map/while/body/eval_jaxpr/ppermute | solution.py:12
  87.9 1.9 %collective-permute-start = (bf16[16,32,128]{2,0,1:T(8,128)(2,1)S(1)}, bf16[16,32,128]{2,0,1:T(8,128)(2,1)S(1)}, u32[]{:S(2)}, u32[]{:S(2)}) collective-permute-start(bf16[16,32,128]{2,0,1:T(8,128)(2,1)S(1)} %broadcast_select_fusion.10), channel_id=1, source_target_pairs={{1,0},{2,1},{3,2},{4,3},{5,4},{6,5},{7,6},{8,7},{9,8},{10,9},{11,1... | collective-permute-start | bytes 393224 | tf_op jit(solution)/shard_map/while/body/eval_jaxpr/ppermute | solution.py:12
  89.9 2.4 %collective-permute-start.1 = (bf16[16,32,128]{2,0,1:T(8,128)(2,1)S(1)}, bf16[16,32,128]{2,0,1:T(8,128)(2,1)S(1)}, u32[]{:S(2)}, u32[]{:S(2)}) collective-permute-start(bf16[16,32,128]{2,0,1:T(8,128)(2,1)S(1)} %broadcast_select_fusion.12), channel_id=1, source_target_pairs={{0,1},{1,2},{2,3},{3,4},{4,5},{5,6},{6,7},{7,8},{8,9},{9,10},{10,1... | collective-permute-start | bytes 393224 | tf_op jit(solution)/shard_map/while/body/eval_jaxpr/ppermute | solution.py:12
  93.0 4.0 %collective-permute-done.1 = bf16[16,32,128]{2,0,1:T(8,128)(2,1)S(1)} collective-permute-done((bf16[16,32,128]{2,0,1:T(8,128)(2,1)S(1)}, bf16[16,32,128]{2,0,1:T(8,128)(2,1)S(1)}, u32[]{:S(2)}, u32[]{:S(2)}) %collective-permute-start.1) | collective-permute-done | bytes 131104 | tf_op jit(solution)/shard_map/while/body/eval_jaxpr/ppermute | solution.py:12
  108.8 2.4 %collective-permute-start.1 = (bf16[16,32,128]{2,0,1:T(8,128)(2,1)S(1)}, bf16[16,32,128]{2,0,1:T(8,128)(2,1)S(1)}, u32[]{:S(2)}, u32[]{:S(2)}) collective-permute-start(bf16[16,32,128]{2,0,1:T(8,128)(2,1)S(1)} %broadcast_select_fusion.12), channel_id=1, source_target_pairs={{0,1},{1,2},{2,3},{3,4},{4,5},{5,6},{6,7},{7,8},{8,9},{9,10},{10,1... | collective-permute-start | bytes 393224 | tf_op jit(solution)/shard_map/while/body/eval_jaxpr/ppermute | solution.py:12
  112.0 4.0 %collective-permute-done.1 = bf16[16,32,128]{2,0,1:T(8,128)(2,1)S(1)} collective-permute-done((bf16[16,32,128]{2,0,1:T(8,128)(2,1)S(1)}, bf16[16,32,128]{2,0,1:T(8,128)(2,1)S(1)}, u32[]{:S(2)}, u32[]{:S(2)}) %collective-permute-start.1) | collective-permute-done | bytes 131104 | tf_op jit(solution)/shard_map/while/body/eval_jaxpr/ppermute | solution.py:12
  127.8 2.4 %collective-permute-start.1 = (bf16[16,32,128]{2,0,1:T(8,128)(2,1)S(1)}, bf16[16,32,128]{2,0,1:T(8,128)(2,1)S(1)}, u32[]{:S(2)}, u32[]{:S(2)}) collective-permute-start(bf16[16,32,128]{2,0,1:T(8,128)(2,1)S(1)} %broadcast_select_fusion.12), channel_id=1, source_target_pairs={{0,1},{1,2},{2,3},{3,4},{4,5},{5,6},{6,7},{7,8},{8,9},{9,10},{10,1... | collective-permute-start | bytes 393224 | tf_op jit(solution)/shard_map/while/body/eval_jaxpr/ppermute | solution.py:12
  131.0 4.0 %collective-permute-done.1 = bf16[16,32,128]{2,0,1:T(8,128)(2,1)S(1)} collective-permute-done((bf16[16,32,128]{2,0,1:T(8,128)(2,1)S(1)}, bf16[16,32,128]{2,0,1:T(8,128)(2,1)S(1)}, u32[]{:S(2)}, u32[]{:S(2)}) %collective-permute-start.1) | collective-permute-done | bytes 131104 | tf_op jit(solution)/shard_map/while/body/eval_jaxpr/ppermute | solution.py:12
  146.7 2.4 %collective-permute-start.1 = (bf16[16,32,128]{2,0,1:T(8,128)(2,1)S(1)}, bf16[16,32,128]{2,0,1:T(8,128)(2,1)S(1)}, u32[]{:S(2)}, u32[]{:S(2)}) collective-permute-start(bf16[16,32,128]{2,0,1:T(8,128)(2,1)S(1)} %broadcast_select_fusion.12), channel_id=1, source_target_pairs={{0,1},{1,2},{2,3},{3,4},{4,5},{5,6},{6,7},{7,8},{8,9},{9,10},{10,1... | collective-permute-start | bytes 393224 | tf_op jit(solution)/shard_map/while/body/eval_jaxpr/ppermute | solution.py:12
  149.9 4.0 %collective-permute-done.1 = bf16[16,32,128]{2,0,1:T(8,128)(2,1)S(1)} collective-permute-done((bf16[16,32,128]{2,0,1:T(8,128)(2,1)S(1)}, bf16[16,32,128]{2,0,1:T(8,128)(2,1)S(1)}, u32[]{:S(2)}, u32[]{:S(2)}) %collective-permute-start.1) | collective-permute-done | bytes 131104 | tf_op jit(solution)/shard_map/while/body/eval_jaxpr/ppermute | solution.py:12
  (375 shorter events, 93.6 us)
Async XLA Ops:
  0.0 164.4 %copy-start = (bf16[256,128]{1,0:T(8,128)(2,1)S(1)}, bf16[256,128]{1,0:T(8,128)(2,1)}, u32[]{:S(2)}) copy-start(bf16[256,128]{1,0:T(8,128)(2,1)} %param.13) | copy-start | bytes 196612
  6.6 2.0 %copy-start.1 = (bf16[2,3,3,256,128]{4,3,2,1,0:T(8,128)(2,1)S(1)}, bf16[2,3,3,256,128]{4,3,2,1,0:T(8,128)(2,1)}, u32[]{:S(2)}) copy-start(bf16[2,3,3,256,128]{4,3,2,1,0:T(8,128)(2,1)} %param.11) | copy-start | bytes 3538948
  8.7 1.8 %copy-start.6 = (s32[4]{0:T(128)S(1)}, s32[4]{0:T(128)}, u32[]{:S(2)}) copy-start(s32[4]{0:T(128)} %param.9) | copy-start | bytes 52
  8.7 2.5 %copy-start.5 = (bf16[1,16,32,128]{3,2,1,0:T(8,128)(2,1)S(1)}, bf16[1,16,32,128]{3,2,1,0:T(8,128)(2,1)}, u32[]{:S(2)}) copy-start(bf16[1,16,32,128]{3,2,1,0:T(8,128)(2,1)} %param.8) | copy-start | bytes 393220
  8.7 2.6 %copy-start.4 = (pred[8,5]{0,1:T(8,128)(4,1)S(1)}, pred[8,5]{0,1:T(8,128)(4,1)}, u32[]{:S(2)}) copy-start(pred[8,5]{0,1:T(8,128)(4,1)} %constant.438) | copy-start | bytes 124
  11.3 5.3 %collective-permute-start = (bf16[16,32,128]{2,0,1:T(8,128)(2,1)S(1)}, bf16[16,32,128]{2,0,1:T(8,128)(2,1)S(1)}, u32[]{:S(2)}, u32[]{:S(2)}) collective-permute-start(bf16[16,32,128]{2,0,1:T(8,128)(2,1)S(1)} %broadcast_select_fusion.10), channel_id=1, source_target_pairs={{1,0},{2,1},{3,2},{4,3},{5,4},{6,5},{7,6},{8,7},{9,8},{10,9},{11,1... | collective-permute-start | bytes 393224 | tf_op jit(solution)/shard_map/while/body/eval_jaxpr/ppermute | solution.py:12
  14.1 7.2 %collective-permute-start.1 = (bf16[16,32,128]{2,0,1:T(8,128)(2,1)S(1)}, bf16[16,32,128]{2,0,1:T(8,128)(2,1)S(1)}, u32[]{:S(2)}, u32[]{:S(2)}) collective-permute-start(bf16[16,32,128]{2,0,1:T(8,128)(2,1)S(1)} %broadcast_select_fusion.12), channel_id=1, source_target_pairs={{0,1},{1,2},{2,3},{3,4},{4,5},{5,6},{6,7},{7,8},{8,9},{9,10},{10,1... | collective-permute-start | bytes 393224 | tf_op jit(solution)/shard_map/while/body/eval_jaxpr/ppermute | solution.py:12
  21.9 1.1 copy-start.2
  24.9 1.1 copy-start.3
  31.1 4.4 %collective-permute-start = (bf16[16,32,128]{2,0,1:T(8,128)(2,1)S(1)}, bf16[16,32,128]{2,0,1:T(8,128)(2,1)S(1)}, u32[]{:S(2)}, u32[]{:S(2)}) collective-permute-start(bf16[16,32,128]{2,0,1:T(8,128)(2,1)S(1)} %broadcast_select_fusion.10), channel_id=1, source_target_pairs={{1,0},{2,1},{3,2},{4,3},{5,4},{6,5},{7,6},{8,7},{9,8},{10,9},{11,1... | collective-permute-start | bytes 393224 | tf_op jit(solution)/shard_map/while/body/eval_jaxpr/ppermute | solution.py:12
  33.0 7.2 %collective-permute-start.1 = (bf16[16,32,128]{2,0,1:T(8,128)(2,1)S(1)}, bf16[16,32,128]{2,0,1:T(8,128)(2,1)S(1)}, u32[]{:S(2)}, u32[]{:S(2)}) collective-permute-start(bf16[16,32,128]{2,0,1:T(8,128)(2,1)S(1)} %broadcast_select_fusion.12), channel_id=1, source_target_pairs={{0,1},{1,2},{2,3},{3,4},{4,5},{5,6},{6,7},{7,8},{8,9},{9,10},{10,1... | collective-permute-start | bytes 393224 | tf_op jit(solution)/shard_map/while/body/eval_jaxpr/ppermute | solution.py:12
  40.8 1.1 copy-start.2
  50.0 4.4 %collective-permute-start = (bf16[16,32,128]{2,0,1:T(8,128)(2,1)S(1)}, bf16[16,32,128]{2,0,1:T(8,128)(2,1)S(1)}, u32[]{:S(2)}, u32[]{:S(2)}) collective-permute-start(bf16[16,32,128]{2,0,1:T(8,128)(2,1)S(1)} %broadcast_select_fusion.10), channel_id=1, source_target_pairs={{1,0},{2,1},{3,2},{4,3},{5,4},{6,5},{7,6},{8,7},{9,8},{10,9},{11,1... | collective-permute-start | bytes 393224 | tf_op jit(solution)/shard_map/while/body/eval_jaxpr/ppermute | solution.py:12
  52.0 7.2 %collective-permute-start.1 = (bf16[16,32,128]{2,0,1:T(8,128)(2,1)S(1)}, bf16[16,32,128]{2,0,1:T(8,128)(2,1)S(1)}, u32[]{:S(2)}, u32[]{:S(2)}) collective-permute-start(bf16[16,32,128]{2,0,1:T(8,128)(2,1)S(1)} %broadcast_select_fusion.12), channel_id=1, source_target_pairs={{0,1},{1,2},{2,3},{3,4},{4,5},{5,6},{6,7},{7,8},{8,9},{9,10},{10,1... | collective-permute-start | bytes 393224 | tf_op jit(solution)/shard_map/while/body/eval_jaxpr/ppermute | solution.py:12
  69.0 4.4 %collective-permute-start = (bf16[16,32,128]{2,0,1:T(8,128)(2,1)S(1)}, bf16[16,32,128]{2,0,1:T(8,128)(2,1)S(1)}, u32[]{:S(2)}, u32[]{:S(2)}) collective-permute-start(bf16[16,32,128]{2,0,1:T(8,128)(2,1)S(1)} %broadcast_select_fusion.10), channel_id=1, source_target_pairs={{1,0},{2,1},{3,2},{4,3},{5,4},{6,5},{7,6},{8,7},{9,8},{10,9},{11,1... | collective-permute-start | bytes 393224 | tf_op jit(solution)/shard_map/while/body/eval_jaxpr/ppermute | solution.py:12
  70.9 7.2 %collective-permute-start.1 = (bf16[16,32,128]{2,0,1:T(8,128)(2,1)S(1)}, bf16[16,32,128]{2,0,1:T(8,128)(2,1)S(1)}, u32[]{:S(2)}, u32[]{:S(2)}) collective-permute-start(bf16[16,32,128]{2,0,1:T(8,128)(2,1)S(1)} %broadcast_select_fusion.12), channel_id=1, source_target_pairs={{0,1},{1,2},{2,3},{3,4},{4,5},{5,6},{6,7},{7,8},{8,9},{9,10},{10,1... | collective-permute-start | bytes 393224 | tf_op jit(solution)/shard_map/while/body/eval_jaxpr/ppermute | solution.py:12
  87.9 4.4 %collective-permute-start = (bf16[16,32,128]{2,0,1:T(8,128)(2,1)S(1)}, bf16[16,32,128]{2,0,1:T(8,128)(2,1)S(1)}, u32[]{:S(2)}, u32[]{:S(2)}) collective-permute-start(bf16[16,32,128]{2,0,1:T(8,128)(2,1)S(1)} %broadcast_select_fusion.10), channel_id=1, source_target_pairs={{1,0},{2,1},{3,2},{4,3},{5,4},{6,5},{7,6},{8,7},{9,8},{10,9},{11,1... | collective-permute-start | bytes 393224 | tf_op jit(solution)/shard_map/while/body/eval_jaxpr/ppermute | solution.py:12
  89.9 7.2 %collective-permute-start.1 = (bf16[16,32,128]{2,0,1:T(8,128)(2,1)S(1)}, bf16[16,32,128]{2,0,1:T(8,128)(2,1)S(1)}, u32[]{:S(2)}, u32[]{:S(2)}) collective-permute-start(bf16[16,32,128]{2,0,1:T(8,128)(2,1)S(1)} %broadcast_select_fusion.12), channel_id=1, source_target_pairs={{0,1},{1,2},{2,3},{3,4},{4,5},{5,6},{6,7},{7,8},{8,9},{9,10},{10,1... | collective-permute-start | bytes 393224 | tf_op jit(solution)/shard_map/while/body/eval_jaxpr/ppermute | solution.py:12
  106.9 4.4 %collective-permute-start = (bf16[16,32,128]{2,0,1:T(8,128)(2,1)S(1)}, bf16[16,32,128]{2,0,1:T(8,128)(2,1)S(1)}, u32[]{:S(2)}, u32[]{:S(2)}) collective-permute-start(bf16[16,32,128]{2,0,1:T(8,128)(2,1)S(1)} %broadcast_select_fusion.10), channel_id=1, source_target_pairs={{1,0},{2,1},{3,2},{4,3},{5,4},{6,5},{7,6},{8,7},{9,8},{10,9},{11,1... | collective-permute-start | bytes 393224 | tf_op jit(solution)/shard_map/while/body/eval_jaxpr/ppermute | solution.py:12
  108.8 7.2 %collective-permute-start.1 = (bf16[16,32,128]{2,0,1:T(8,128)(2,1)S(1)}, bf16[16,32,128]{2,0,1:T(8,128)(2,1)S(1)}, u32[]{:S(2)}, u32[]{:S(2)}) collective-permute-start(bf16[16,32,128]{2,0,1:T(8,128)(2,1)S(1)} %broadcast_select_fusion.12), channel_id=1, source_target_pairs={{0,1},{1,2},{2,3},{3,4},{4,5},{5,6},{6,7},{7,8},{8,9},{9,10},{10,1... | collective-permute-start | bytes 393224 | tf_op jit(solution)/shard_map/while/body/eval_jaxpr/ppermute | solution.py:12
  125.8 4.4 %collective-permute-start = (bf16[16,32,128]{2,0,1:T(8,128)(2,1)S(1)}, bf16[16,32,128]{2,0,1:T(8,128)(2,1)S(1)}, u32[]{:S(2)}, u32[]{:S(2)}) collective-permute-start(bf16[16,32,128]{2,0,1:T(8,128)(2,1)S(1)} %broadcast_select_fusion.10), channel_id=1, source_target_pairs={{1,0},{2,1},{3,2},{4,3},{5,4},{6,5},{7,6},{8,7},{9,8},{10,9},{11,1... | collective-permute-start | bytes 393224 | tf_op jit(solution)/shard_map/while/body/eval_jaxpr/ppermute | solution.py:12
  127.8 7.2 %collective-permute-start.1 = (bf16[16,32,128]{2,0,1:T(8,128)(2,1)S(1)}, bf16[16,32,128]{2,0,1:T(8,128)(2,1)S(1)}, u32[]{:S(2)}, u32[]{:S(2)}) collective-permute-start(bf16[16,32,128]{2,0,1:T(8,128)(2,1)S(1)} %broadcast_select_fusion.12), channel_id=1, source_target_pairs={{0,1},{1,2},{2,3},{3,4},{4,5},{5,6},{6,7},{7,8},{8,9},{9,10},{10,1... | collective-permute-start | bytes 393224 | tf_op jit(solution)/shard_map/while/body/eval_jaxpr/ppermute | solution.py:12
  144.8 4.4 %collective-permute-start = (bf16[16,32,128]{2,0,1:T(8,128)(2,1)S(1)}, bf16[16,32,128]{2,0,1:T(8,128)(2,1)S(1)}, u32[]{:S(2)}, u32[]{:S(2)}) collective-permute-start(bf16[16,32,128]{2,0,1:T(8,128)(2,1)S(1)} %broadcast_select_fusion.10), channel_id=1, source_target_pairs={{1,0},{2,1},{3,2},{4,3},{5,4},{6,5},{7,6},{8,7},{9,8},{10,9},{11,1... | collective-permute-start | bytes 393224 | tf_op jit(solution)/shard_map/while/body/eval_jaxpr/ppermute | solution.py:12
  146.7 7.2 %collective-permute-start.1 = (bf16[16,32,128]{2,0,1:T(8,128)(2,1)S(1)}, bf16[16,32,128]{2,0,1:T(8,128)(2,1)S(1)}, u32[]{:S(2)}, u32[]{:S(2)}) collective-permute-start(bf16[16,32,128]{2,0,1:T(8,128)(2,1)S(1)} %broadcast_select_fusion.12), channel_id=1, source_target_pairs={{0,1},{1,2},{2,3},{3,4},{4,5},{5,6},{6,7},{7,8},{8,9},{9,10},{10,1... | collective-permute-start | bytes 393224 | tf_op jit(solution)/shard_map/while/body/eval_jaxpr/ppermute | solution.py:12
  (13 other events, 13.8 us)
